TPU v7x, 32 devices: a whole 2x2x4 slice. The times are simulated.
32 devices in a mesh: region: 4 (over y, x), tile: 8 (over z, core).
Axes of the slice: x: 2, y: 2, z: 4, core: 2. Of those that a mesh axis runs over, the one named last changes fastest.
Arguments:
- estimate: float32 [32, 128, 512], P('region', 'tile'), may hold values from 0.5 to 18
- observed: float32 [32, 16, 32, 512], P('region', 'tile'), may hold values from 0.3 to 3
- tile_offset: int32 [16], P('tile'), may hold values from 0 to 96
- tile_view: int32 [16], P('tile'), may hold values from 0 to 5
- psf_taps: float32 [6, 3, 3, 15], replicated, may hold values from 0.01 to 0.1
- view_weight: float32 [6], replicated, may hold values from 0.5 to 2
Outputs:
- updated: float32 [32, 128, 512], P('region', 'tile')
All inputs are finite; a program needn't handle non-finite values.
Results may differ from a plain program's by a relative error of at most 0.0003.
Values sent between devices are 32-bit elements; how exact they have to be, the bound alone decides.
No kernel may reach another device: no remote copies, remote signals or barrier semaphores. Data moves between devices by JAX's collectives and lax.ppermute only.
A program may use at most 128 MiB of HBM per device.

v0:
```python
import jax
import jax.numpy as jnp
from jax import lax
from jax.sharding import PartitionSpec as P

PRIOR_WEIGHT = 0.25
MATMUL_PRECISION = lax.Precision.HIGH


def with_halo(cells, sides, width):
    for axis, dim in sides:
        count = lax.axis_size(axis)
        ends = count - 1
        head = lax.slice_in_dim(cells, 0, width, axis=dim)
        tail = lax.slice_in_dim(cells, cells.shape[dim] - width, cells.shape[dim], axis=dim)
        cells = jnp.concatenate(
            [
                lax.ppermute(tail, axis, [(i, (i + 1) % count) for i in range(ends)]),
                cells,
                lax.ppermute(head, axis, [((i + 1) % count, i) for i in range(ends)]),
            ],
            axis=dim,
        )
    return cells


def band(taps, rows, cols, shift):
    kt = taps.shape[-1]
    i = lax.broadcasted_iota(jnp.int32, (rows, cols), 0)
    j = lax.broadcasted_iota(jnp.int32, (rows, cols), 1)
    d = j - i - jnp.asarray(shift, jnp.int32)[..., None, None]
    out = jnp.zeros(d.shape[:-2] + (rows, cols), jnp.float32)
    out = jnp.broadcast_to(out, taps.shape[:-1] + (rows, cols))
    for k in range(kt):
        out = jnp.where(d == k, taps[..., k, None, None], out)
    return out


def kron_band(taps_a, taps_b, rows_a, rows_b, span_b, cols, shift_a, shift_b):
    kt = taps_a.shape[-1]
    lead = taps_a.shape[:-1]
    ia = lax.broadcasted_iota(jnp.int32, (rows_a, cols), 0)
    ca = lax.broadcasted_iota(jnp.int32, (rows_a, cols), 1) // span_b
    ib = lax.broadcasted_iota(jnp.int32, (rows_b, cols), 0)
    cb = lax.broadcasted_iota(jnp.int32, (rows_b, cols), 1) % span_b
    da = ca - ia - jnp.asarray(shift_a, jnp.int32)[..., None, None]
    db = cb - ib - jnp.asarray(shift_b, jnp.int32)[..., None, None]
    ea = jnp.zeros(lead + (rows_a, cols), jnp.float32)
    eb = jnp.zeros(lead + (rows_b, cols), jnp.float32)
    for k in range(kt):
        ea = jnp.where(da == k, taps_a[..., k, None, None], ea)
        eb = jnp.where(db == k, taps_b[..., k, None, None], eb)
    return ea[..., :, None, :] * eb[..., None, :, :]


def depth_band(taps, depth, block):
    kt = taps.shape[-1]
    half = (kt - 1) // 2
    i = lax.broadcasted_iota(jnp.int32, (3 * block, block), 0)
    j = lax.broadcasted_iota(jnp.int32, (3 * block, block), 1)
    d = i - block - j + half
    strip = jnp.zeros(taps.shape[:-1] + (3 * block, block), jnp.float32)
    for k in range(kt):
        strip = jnp.where(d == k, taps[..., k, None, None], strip)
    nb = depth // block
    lead = taps.shape[:-1]
    cols = []
    for b in range(nb):
        col = jnp.pad(strip, [(0, 0)] * len(lead) + [(b * block, (nb - 1 - b) * block), (0, 0)])
        cols.append(col[..., block : block + depth, :])
    return jnp.concatenate(cols, axis=-1)


def on_device(estimate, observed, tile_offset, tile_view, psf_taps, view_weight):
    kt = psf_taps.shape[3]
    rim = (kt - 1) // 2
    block_x, block_y, depth = estimate.shape
    tile_count = observed.shape[1]
    tile_rows = observed.shape[2]
    rank_terms = psf_taps.shape[1]
    group_size = lax.axis_size("tile")
    region_rows = block_y * group_size
    win_rows = -(-(tile_rows + 2 * rim) // 8) * 8
    win_x = block_x + 2 * rim
    tile_info = jnp.stack([tile_offset.astype(jnp.float32), view_weight[tile_view]], axis=1)
    all_info = lax.all_gather(tile_info, "tile", tiled=True)
    all_offset = all_info[:, 0].astype(jnp.int32)
    all_weight = all_info[:, 1]
    core = lax.all_gather(estimate, "tile", axis=1, tiled=True)
    count = lax.axis_size("region")
    lower = lax.ppermute(
        estimate[block_x - rim :], "region", [(i, i + 1) for i in range(count - 1)]
    )
    upper = lax.ppermute(estimate[:rim], "region", [(i + 1, i) for i in range(count - 1)])
    rims = lax.all_gather(jnp.concatenate([lower, upper], axis=0), "tile", axis=1, tiled=True)
    gathered = jnp.concatenate([rims[:rim], core, rims[rim:]], axis=0)
    filters = psf_taps[tile_view]
    weight = view_weight[tile_view]
    ax = filters[:, :, 0]
    ay = filters[:, :, 1]
    az = filters[:, :, 2]
    starts = jnp.clip(tile_offset - rim, 0, region_rows - win_rows)
    shifts = tile_offset - rim - starts
    windows = jnp.stack(
        [lax.dynamic_slice_in_dim(gathered, starts[j], win_rows, 1) for j in range(tile_count)]
    ).reshape(tile_count, win_x * win_rows, depth)
    kxy = kron_band(
        ax, ay, block_x, tile_rows, win_rows, win_x * win_rows, 0, shifts[:, None]
    ).reshape(tile_count, rank_terms * block_x * tile_rows, win_x * win_rows)
    tz = depth_band(az, depth, 128)
    cells = block_x * tile_rows
    part = jnp.einsum("tmk,tkz->tmz", kxy, windows, precision=MATMUL_PRECISION)
    part = part.reshape(tile_count, rank_terms, cells, depth)
    blurred = jnp.einsum("tqmz,tqzn->tmn", part, tz, precision=MATMUL_PRECISION)
    quotient = observed.transpose(1, 0, 2, 3).reshape(tile_count, cells, depth) / blurred
    fxy = kron_band(
        ax[..., ::-1], ay[..., ::-1], block_x, tile_rows, tile_rows, cells, -rim, -rim
    ).reshape(tile_count, rank_terms * cells, cells)
    part = jnp.einsum("tmk,tkz->tmz", fxy, quotient, precision=MATMUL_PRECISION)
    part = part.reshape(tile_count, rank_terms, cells, depth)
    correction = jnp.einsum("tqmz,tqnz->tmn", part, tz, precision=MATMUL_PRECISION)
    weighted = (weight[:, None, None] * correction).reshape(tile_count, block_x, tile_rows, depth)
    numerator = jnp.zeros((block_x, region_rows, depth), jnp.float32)
    for j in range(tile_count):
        current = lax.dynamic_slice_in_dim(numerator, tile_offset[j], tile_rows, 1)
        numerator = lax.dynamic_update_slice_in_dim(
            numerator, current + weighted[j], tile_offset[j], 1
        )
    own_numerator = lax.psum_scatter(numerator, "tile", scatter_dimension=1, tiled=True)
    me = lax.axis_index("tile")
    rows = me * block_y + jnp.arange(block_y, dtype=jnp.int32)
    inside = (rows[None, :] >= all_offset[:, None]) & (
        rows[None, :] < all_offset[:, None] + tile_rows
    )
    own_coverage = jnp.sum(jnp.where(inside, all_weight[:, None], 0.0), axis=0)
    return estimate * (own_numerator + PRIOR_WEIGHT) / (own_coverage[None, :, None] + PRIOR_WEIGHT)


def solution(mesh):
    return jax.shard_map(
        on_device,
        mesh=mesh,
        in_specs=(
            P("region", "tile", None),
            P("region", "tile", None, None),
            P("tile"),
            P("tile"),
            P(),
            P(),
        ),
        out_specs=P("region", "tile", None),
        check_vma=False,
    )
```

profile of v0, /device:TPU:0, one launch (start us, length us, event | category | flops | bytes accessed | tf_op | source)
XLA Modules:
  0.0 163.6 jit_solution(2711943102630633958)
XLA Ops:
  6.5 1.1 fusion.82
  7.7 4.9 %collective-permute-start = (f32[7,16,512]{2,1,0:T(8,128)S(1)}, f32[7,16,512]{2,1,0:T(8,128)S(1)}, u32[]{:S(2)}, u32[]{:S(2)}) collective-permute-start(f32[7,16,512]{2,1,0:T(8,128)S(1)} %get-tuple-element.15), channel_id=1, source_target_pairs={{0,8},{8,16},{16,24},{1,9},{9,17},{17,25},{2,10},{10,18},{18,26},{... | collective-permute-start | bytes 688136 | tf_op jit(solution)/shard_map/ppermute | solution.py:91
  12.5 1.3 collective-permute-start.1
  13.8 3.5 %collective-permute-done = f32[7,16,512]{2,1,0:T(8,128)S(1)} collective-permute-done((f32[7,16,512]{2,1,0:T(8,128)S(1)}, f32[7,16,512]{2,1,0:T(8,128)S(1)}, u32[]{:S(2)}, u32[]{:S(2)}) %collective-permute-start) | collective-permute-done | bytes 229408 | tf_op jit(solution)/shard_map/ppermute | solution.py:91
  17.4 6.9 %collective-permute-done.1 = f32[7,16,512]{2,1,0:T(8,128)S(1)} collective-permute-done((f32[7,16,512]{2,1,0:T(8,128)S(1)}, f32[7,16,512]{2,1,0:T(8,128)S(1)}, u32[]{:S(2)}, u32[]{:S(2)}) %collective-permute-start.1) | collective-permute-done | bytes 229408 | tf_op jit(solution)/shard_map/ppermute | solution.py:94
  24.2 0.8 pad_maximum_fusion.12
  25.1 0.7 all-gather.6.cloned.1.call-update
  25.9 0.7 fusion.89
  29.3 0.6 fusion.88
  32.3 0.6 gather_fusion.1
  32.9 0.1 fusion.87
  33.0 0.1 copy.178
  33.1 0.1 copy.179
  33.2 0.1 copy.180
  33.3 0.1 copy.181
  33.4 0.1 copy.182
  33.5 0.1 copy.183
  34.1 0.1 copy.189
  34.2 0.1 copy.190
  34.3 0.1 copy.191
  34.4 0.1 copy.192
  34.5 0.1 fusion.86
  34.6 0.1 copy.162
  34.8 0.1 copy.172
  34.9 0.1 copy.173
  35.0 0.1 copy.174
  35.1 0.1 copy.175
  35.2 0.1 copy.176
  35.3 0.1 copy.163
  35.4 0.1 copy.164
  35.5 0.1 copy.165
  35.6 0.1 copy.166
  36.1 0.1 fusion.85
  36.2 0.1 copy.196
  37.7 0.6 fusion.23
  38.3 1.5 select_select_fusion
  39.8 2.9 %pad_slice_fusion.3 = (f32[2,3,512,128]{3,2,1,0:T(8,128)}, f32[2,3,512,128]{3,2,1,0:T(8,128)}, f32[2,3,512,128]{3,2,1,0:T(8,128)}, f32[2,3,512,128]{3,2,1,0:T(8,128)}) fusion(f32[2,3,384,128]{3,2,1,0:T(8,128)S(1)} %select_select_fusion), kind=kLoop, calls=%fused_computation.14 | loop fusion | bytes 7471104 | tf_op jit(solution)/shard_map/slice | solution.py:70
  42.7 1.1 copy.193
  43.8 0.6 gather_fusion
  45.9 0.4 select_select_fusion.3
  46.2 0.2 select_select_fusion.4
  46.4 0.2 broadcast_multiply_fusion.1
  47.9 0.4 select_select_fusion.2
  48.3 0.7 subtract_compare_fusion.14
  49.0 1.4 select_select_fusion.1
  50.4 3.7 %broadcast_multiply_fusion = f32[2,3,8,32,1056]{4,3,2,1,0:T(8,128)} fusion(f32[2,3,32,1056]{3,2,1,0:T(8,128)S(1)} %select_select_fusion.1, f32[2,3,8,1056]{3,2,1,0:T(8,128)S(1)} %select_select_fusion.2), kind=kLoop, calls=%fused_computation.10 | loop fusion | flops 1622016 | bytes 7501824 | tf_op jit(solution)/shard_map/mul | solution.py:53
  54.1 13.9 %all-gather.4.cloned.1.call-done = f32[14,128,512]{2,1,0:T(8,128)} async-done(((f32[14,16,512]{2,1,0:T(8,128)}), f32[14,128,512]{2,1,0:T(8,128)}) %all-gather.4.cloned.1.call-update) | async-done | bytes 3670032 | tf_op jit(solution)/shard_map/all_gather | solution.py:95
  68.1 3.8 %fusion.80 = (f32[7,128,512]{2,1,0:T(8,128)S(1)}, f32[7,128,512]{2,1,0:T(8,128)}) fusion(f32[14,128,512]{2,1,0:T(8,128)} %all-gather.4.cloned.1.call-done), kind=kLoop, calls=%fused_computation.146 | loop fusion | bytes 7340032 | tf_op jit(solution)/shard_map/slice | solution.py:96
  71.9 25.8 %all-gather.6.cloned.1.call-done = f32[8,128,512]{2,1,0:T(8,128)} async-done(((f32[8,16,512]{2,1,0:T(8,128)}), f32[8,128,512]{2,1,0:T(8,128)}) %all-gather.6.cloned.1.call-update) | async-done | bytes 2097168 | tf_op jit(solution)/shard_map/all_gather | solution.py:89
  97.7 3.0 %pad_maximum_fusion.1 = f32[22,128,512]{2,1,0:T(8,128)S(1)} fusion(f32[7,128,512]{2,1,0:T(8,128)} %get-tuple-element.8, f32[8,128,512]{2,1,0:T(8,128)} %all-gather.6.cloned.1.call-done, f32[7,128,512]{2,1,0:T(8,128)S(1)} %get-tuple-element.7), kind=kLoop, calls=%fused_computation.3 | loop fusion | flops 2883584 | bytes 11534336 | tf_op jit(solution)/shard_map/concatenate | solution.py:96
  100.7 0.8 constant_dynamic-slice_fusion.1
  101.5 0.5 slice-done.1
  102.0 6.6 %fusion = f32[2,768,512]{2,1,0:T(8,128)S(1)} fusion(f32[2,768,1056]{2,1,0:T(8,128)S(1)} %bitcast.97, f32[1,1056,512]{2,1,0:T(8,128)S(1)} %bitcast.100, f32[1,1056,512]{2,1,0:T(8,128)S(1)} %bitcast.99), kind=kOutput, calls=%fused_computation.4 | convolution fusion | flops 4983914496 | bytes 13959168 | tf_op jit(solution)/shard_map/tmk,tkz->tmz/dot_general | solution.py:112
  108.7 3.3 %bitcast_divide_fusion = f32[2,256,512]{2,1,0:T(8,128)S(1)} fusion(f32[8,2,32,512]{3,2,0,1:T(8,128)S(1)} %copy-done.9, f32[2,3,256,512]{3,2,1,0:T(8,128)S(1)} %bitcast.102, f32[2,3,512,128]{3,2,1,0:T(8,128)S(1)} %copy-done.4, f32[2,3,512,128]{3,2,1,0:T(8,128)S(1)} %copy-done.5, f32[2,3,512,128]{3,2,1,0:T(8,128)S(1)} %copy-done.6, ...), kind=kOutput, calls=%fused_computation.34 | convolution fusion | flops 2420899840 | bytes 11534336 | tf_op jit(solution)/shard_map/tqmz,tqzn->tmn/dot_general | solution.py:114
  112.0 1.5 fusion.90
  113.5 3.0 %fusion.8 = f32[2,256,512]{2,1,0:T(8,128)S(1)} fusion(f32[2,3,256,512]{3,2,1,0:T(8,128)S(1)} %bitcast.98, f32[2,3,512,128]{3,2,1,0:T(8,128)S(1)} %copy-done.4, f32[2,3,512,128]{3,2,1,0:T(8,128)S(1)} %copy-done.5, f32[2,3,512,128]{3,2,1,0:T(8,128)S(1)} %copy-done.6, f32[2,3,512,128]{3,2,1,0:T(8,128)S(1)} %copy-done.3, f32[2]{0:T(128)S(1)} %gather_fusion), kind=kOutput, calls=%fused_computation.32 | convolution fusion | flops 2420899840 | bytes 10485768 | tf_op jit(solution)/shard_map/tqmz,tqnz->tmn/dot_general | solution.py:121
  116.6 0.2 broadcast_in_dim.790
  116.9 0.7 dynamic_update_slice.6
  117.6 0.1 dynamic-slice_add_fusion
  117.7 0.7 dynamic_update_slice.7
  118.5 1.3 copy-done.2
  120.0 10.4 %all-gather = f32[8,2,2]{2,1,0:T(2,128)S(1)} all-gather(f32[1,2,2]{2,1,0:T(2,128)S(1)} %bitcast.185), channel_id=1, replica_groups=mesh['region'=4,'tile'=8] {'tile'}, dimensions={0}, use_global_device_ids=true | all-gather | bytes 144 | tf_op jit(solution)/shard_map/all_gather | solution.py:86
  130.8 24.6 %reduce-scatter.2.cloned.1.call-done = f32[8,16,512]{2,1,0:T(8,128)} async-done(((f32[8,128,512]{2,1,0:T(8,128)}), f32[8,16,512]{2,1,0:T(8,128)}) %reduce-scatter.2.cloned.1.call-update) | async-done | bytes 262160 | tf_op jit(solution)/shard_map/reduce_scatter | solution.py:129
  155.3 1.8 %multiply_divide_fusion = f32[8,16,512]{2,1,0:T(8,128)} fusion(f32[8,16,512]{2,1,0:T(8,128)S(1)} %copy-done.7, f32[8,16,512]{2,1,0:T(8,128)} %reduce-scatter.2.cloned.1.call-done, f32[16]{0:T(128)S(1)} %broadcast_add_fusion.2), kind=kLoop, calls=%fused_computation.39 | loop fusion | flops 196608 | bytes 786496 | tf_op jit(solution)/shard_map/div | solution.py:136
  (85 shorter events, 3.3 us)
Async XLA Ops:
  6.5 25.8 %copy-start = (f32[6,3,3,15]{3,2,1,0:T(4,128)S(1)}, f32[6,3,3,15]{3,2,1,0:T(4,128)}, u32[]{:S(2)}) copy-start(f32[6,3,3,15]{3,2,1,0:T(4,128)} %param.10) | copy-start | bytes 9724
  6.5 19.4 %copy-start.10 = (s32[2]{0:T(128)S(1)}, s32[2]{0:T(128)}, u32[]{:S(2)}) copy-start(s32[2]{0:T(128)} %param.8) | copy-start | bytes 28
  6.5 19.4 %copy-start.11 = (s32[2]{0:T(128)S(1)}, s32[2]{0:T(128)}, u32[]{:S(2)}) copy-start(s32[2]{0:T(128)} %param.9) | copy-start | bytes 28
  6.5 61.6 %all-gather.4.cloned.1.call-start = ((), (), s32[]{:S(2)}) async-start(), calls=%async_computation.1 | async-start | bytes 4128768 | tf_op jit(solution)/shard_map/all_gather | solution.py:95
  7.7 9.7 %collective-permute-start = (f32[7,16,512]{2,1,0:T(8,128)S(1)}, f32[7,16,512]{2,1,0:T(8,128)S(1)}, u32[]{:S(2)}, u32[]{:S(2)}) collective-permute-start(f32[7,16,512]{2,1,0:T(8,128)S(1)} %get-tuple-element.15), channel_id=1, source_target_pairs={{0,8},{8,16},{16,24},{1,9},{9,17},{17,25},{2,10},{10,18},{18,26},{... | collective-permute-start | bytes 688136 | tf_op jit(solution)/shard_map/ppermute | solution.py:91
  12.5 11.7 %collective-permute-start.1 = (f32[7,16,512]{2,1,0:T(8,128)S(1)}, f32[7,16,512]{2,1,0:T(8,128)S(1)}, u32[]{:S(2)}, u32[]{:S(2)}) collective-permute-start(f32[7,16,512]{2,1,0:T(8,128)S(1)} %get-tuple-element.16), channel_id=1, source_target_pairs={{8,0},{16,8},{24,16},{9,1},{17,9},{25,17},{10,2},{18,10},{26,18},{... | collective-permute-start | bytes 688136 | tf_op jit(solution)/shard_map/ppermute | solution.py:94
  25.0 72.7 %all-gather.6.cloned.1.call-start = ((), (), s32[]{:S(2)}) async-start(), calls=%async_computation.2 | async-start | bytes 2359296 | tf_op jit(solution)/shard_map/all_gather | solution.py:89
  25.8 129.5 %reduce-scatter.2.cloned.1.call-start = ((), (), s32[]{:S(2)}) async-start(), calls=%async_computation.3 | async-start | bytes 2359296 | tf_op jit(solution)/shard_map/reduce_scatter | solution.py:129
  39.8 2.9 %copy-start.8 = (f32[8,2,32,512]{3,2,1,0:T(8,128)S(1)}, f32[8,2,32,512]{3,2,1,0:T(8,128)}, u32[]{:S(2)}) copy-start(f32[8,2,32,512]{3,2,1,0:T(8,128)} %param.7) | copy-start | bytes 3145732
  42.7 1.1 copy-start.1
  97.7 3.8 %slice-start = ((s8[7077888]{0:T(1024)(128)(4,1)}), s8[4194304]{0:T(1024)(128)(4,1)S(1)}, s32[]{:S(2)}) async-start(s8[7077888]{0:T(1024)(128)(4,1)} %bitcast.95), calls=%async_computation.4 | async-start | bytes 8388608
  97.7 4.3 %slice-start.1 = ((s8[7077888]{0:T(1024)(128)(4,1)}), s8[2883584]{0:T(1024)(128)(4,1)S(1)}, s32[]{:S(2)}) async-start(s8[7077888]{0:T(1024)(128)(4,1)} %bitcast.95), calls=%async_computation.5 | async-start | bytes 5767168
  102.0 6.6 %copy-start.3 = (f32[2,3,512,128]{3,2,1,0:T(8,128)S(1)}, f32[2,3,512,128]{3,2,1,0:T(8,128)}, u32[]{:S(2)}) copy-start(f32[2,3,512,128]{3,2,1,0:T(8,128)} %get-tuple-element.9) | copy-start | bytes 4718596
  102.0 6.7 %copy-start.4 = (f32[2,3,512,128]{3,2,1,0:T(8,128)S(1)}, f32[2,3,512,128]{3,2,1,0:T(8,128)}, u32[]{:S(2)}) copy-start(f32[2,3,512,128]{3,2,1,0:T(8,128)} %get-tuple-element.10) | copy-start | bytes 4718596
  102.0 6.7 %copy-start.5 = (f32[2,3,512,128]{3,2,1,0:T(8,128)S(1)}, f32[2,3,512,128]{3,2,1,0:T(8,128)}, u32[]{:S(2)}) copy-start(f32[2,3,512,128]{3,2,1,0:T(8,128)} %get-tuple-element.11) | copy-start | bytes 4718596
  102.0 6.7 %copy-start.6 = (f32[2,3,512,128]{3,2,1,0:T(8,128)S(1)}, f32[2,3,512,128]{3,2,1,0:T(8,128)}, u32[]{:S(2)}) copy-start(f32[2,3,512,128]{3,2,1,0:T(8,128)} %get-tuple-element.12) | copy-start | bytes 4718596
  102.0 6.7 %copy-start.9 = (f32[8,2,32,512]{3,2,0,1:T(8,128)S(1)}, f32[8,2,32,512]{3,2,0,1:T(8,128)}, u32[]{:S(2)}) copy-start(f32[8,2,32,512]{3,2,0,1:T(8,128)} %copy.193) | copy-start | bytes 3145732
  117.7 37.6 %copy-start.7 = (f32[8,16,512]{2,1,0:T(8,128)S(1)}, f32[8,16,512]{2,1,0:T(8,128)}, u32[]{:S(2)}) copy-start(f32[8,16,512]{2,1,0:T(8,128)} %param.6) | copy-start | bytes 786436
  118.5 1.4 copy-start.2
Sparse Core Ops, SparseCore 0:
  25.2 42.8 all-gather.3
  69.7 27.9 all-gather.5
  120.0 35.2 reduce-scatter.1
where the time goes:
time: 164 us
  waiting for transfers between devices  75.4 us (46%)
  between operations  21.2 us (13%)
  local copies, waits for them, and re-layouts  20.8 us (13%)
  other arithmetic  15 us (9%)
  matrix products  14.4 us (9%)
  blocking collectives  10.4 us (6%)
  starting transfers between devices  6.23 us (4%)
    all_gather x1, waiting for transfers between devices, on_device(): core = lax.all_gather(estimate, 'tile', axis=1, tiled=True)  25.8 us
    reduce_scatter x1, waiting for transfers between devices, on_device(): lax.psum_scatter(numerator, 'tile', scatter_dimension=1, tiled=True)  24.6 us
    all_gather x1, waiting for transfers between devices, on_device(): lax.all_gather(jnp.concatenate([lower, upper], axis=0), 'tile', axis=1, t...  13.9 us
    all_gather x1, blocking collectives, on_device(): all_info = lax.all_gather(tile_info, 'tile', tiled=True)  10.4 us
    ppermute x1, waiting for transfers between devices, on_device(): lax.ppermute(estimate[:rim], 'region', [(i + 1, i) for i in range(count -...  6.86 us
    dot_general x1, matrix products, on_device(): part = jnp.einsum('tmk,tkz->tmz', kxy, windows, precision=MATMUL_PRECISION)  6.62 us
    ppermute x1, starting transfers between devices, on_device(): lax.ppermute(estimate[block_x - rim:], 'region', [(i, i + 1) for i in ran...  4.86 us
    mul x2, other arithmetic, kron_band(): return ea[..., :, None, :] * eb[..., None, :, :]  3.9 us
  transfers between devices with their start and end apart: 5, of which 5 were waited for; matrix products, arithmetic and copies ran while one was open for 15% of the time, Pallas kernels for 0%

commit v1 on v0

--- a/solution.py
+++ b/solution.py
@@ -5,6 +5,28 @@
 
 PRIOR_WEIGHT = 0.25
 MATMUL_PRECISION = lax.Precision.HIGH
+
+
+def laid_out(blocks, dim):
+    lengths = list(blocks.shape[1:])
+    lengths[dim] *= blocks.shape[0]
+    return jnp.moveaxis(blocks, 0, dim).reshape(lengths)
+
+
+def collected_by_bits(x, axis):
+    length = lax.axis_size(axis)
+    pieces = x[None]
+    for level in range(length.bit_length() - 1):
+        bit = 1 << level
+        theirs = lax.ppermute(pieces, axis, [(i, i ^ bit) for i in range(length)])
+        both = jnp.stack([pieces, theirs])
+        upper = lax.axis_index(axis) >> level & 1
+        pieces = jnp.where(upper == 0, both, both[::-1]).reshape(-1, *x.shape)
+    return pieces
+
+
+def gather_by_bits(x, axis, dim):
+    return laid_out(collected_by_bits(x, axis), dim)
 
 
 def with_halo(cells, sides, width):
@@ -92,7 +114,7 @@
         estimate[block_x - rim :], "region", [(i, i + 1) for i in range(count - 1)]
     )
     upper = lax.ppermute(estimate[:rim], "region", [(i + 1, i) for i in range(count - 1)])
-    rims = lax.all_gather(jnp.concatenate([lower, upper], axis=0), "tile", axis=1, tiled=True)
+    rims = gather_by_bits(jnp.concatenate([lower, upper], axis=0), "tile", 1)
     gathered = jnp.concatenate([rims[:rim], core, rims[rim:]], axis=0)
     filters = psf_taps[tile_view]
     weight = view_weight[tile_view]

time: 164 us -> 220 us (1.34)
  waiting for transfers between devices: 75.4 us -> 121 us
  starting transfers between devices: 6.23 us -> 11.2 us
  other arithmetic: 15 us -> 18.1 us
    ppermute x0 -> x3, waiting for transfers between devices: none -> 94.2 us  [collected_by_bits(): theirs = lax.ppermute(pieces, axis, [(i, i ^ bit) for i in range(length)])]
    all_gather x1, waiting for transfers between devices: 25.8 us -> 0.01 us  [on_device(): core = lax.all_gather(estimate, 'tile', axis=1, tiled=True)]
    all_gather x1 -> x0, waiting for transfers between devices: 13.9 us -> none  [on_device(): lax.all_gather(jnp.concatenate([lower, upper], axis=0), 'tile', axis=1, t...]
    ppermute x1, waiting for transfers between devices: 6.86 us -> 0.01 us  [on_device(): lax.ppermute(estimate[:rim], 'region', [(i + 1, i) for i in range(count -...]
    ppermute x0 -> x3, starting transfers between devices: none -> 4.37 us  [collected_by_bits(): theirs = lax.ppermute(pieces, axis, [(i, i ^ bit) for i in range(length)])]
    ppermute x1, waiting for transfers between devices: 3.53 us -> 0.01 us  [on_device(): lax.ppermute(estimate[block_x - rim:], 'region', [(i, i + 1) for i in ran...]
  transfers between devices with their start and end apart: 5 -> 7, of which waited for: 5 -> 3; matrix products, arithmetic and copies ran while one was open for 15% -> 14% of each run, Pallas kernels for 0% -> 0%
where the time goes in v1:
time: 220 us; the launch traced here: 219 us
  waiting for transfers between devices  121 us (55%)
  local copies, waits for them, and re-layouts  21.5 us (10%)
  between operations  21.2 us (10%)
  other arithmetic  18.1 us (8%)
  matrix products  14.5 us (7%)
  blocking collectives  11.9 us (5%)
  starting transfers between devices  11.2 us (5%)
    ppermute x3, waiting for transfers between devices, collected_by_bits(): theirs = lax.ppermute(pieces, axis, [(i, i ^ bit) for i in range(length)])  94.2 us
    reduce_scatter x1, waiting for transfers between devices, on_device(): lax.psum_scatter(numerator, 'tile', scatter_dimension=1, tiled=True)  25.9 us
    all_gather x1, blocking collectives, on_device(): all_info = lax.all_gather(tile_info, 'tile', tiled=True)  11.9 us
    dot_general x1, matrix products, on_device(): part = jnp.einsum('tmk,tkz->tmz', kxy, windows, precision=MATMUL_PRECISION)  6.63 us
    ppermute x1, starting transfers between devices, on_device(): lax.ppermute(estimate[block_x - rim:], 'region', [(i, i + 1) for i in ran...  5.55 us
  transfers between devices with their start and end apart: 7, of which 3 were waited for; matrix products, arithmetic and copies ran while one was open for 14% of the time, Pallas kernels for 0%

profile of v1, /device:TPU:0, one launch (start us, length us, event | category | flops | bytes accessed | tf_op | source)
XLA Modules:
  0.0 219.1 jit_solution(18091535045841831435)
XLA Ops:
  6.5 0.7 all-gather.3.cloned.1.call-update
  7.3 1.1 fusion.84
  8.4 5.5 %collective-permute-start = (f32[7,16,512]{2,1,0:T(8,128)S(1)}, f32[7,16,512]{2,1,0:T(8,128)}, u32[]{:S(2)}, u32[]{:S(2)}) collective-permute-start(f32[7,16,512]{2,1,0:T(8,128)S(1)} %get-tuple-element.18), channel_id=1, source_target_pairs={{0,8},{8,16},{16,24},{1,9},{9,17},{17,25},{2,10},{10,18},{18,26},{... | collective-permute-start | bytes 688136 | tf_op jit(solution)/shard_map/ppermute | solution.py:113
  13.9 1.3 collective-permute-start.1
  15.3 1.3 fusion.90
  16.6 0.7 convert_bitcast_fusion.1
  17.4 0.6 gather_fusion.1
  17.9 0.1 fusion.89
  18.1 0.1 copy.181
  18.2 0.1 copy.182
  18.3 0.1 copy.183
  18.4 0.1 copy.184
  18.5 0.1 copy.185
  18.6 0.1 copy.186
  18.7 0.1 copy.187
  18.7 0.1 copy.188
  18.8 0.1 copy.189
  18.9 0.1 copy.190
  19.5 0.1 fusion.88
  19.7 0.1 copy.165
  21.1 0.1 fusion.87
  21.3 0.1 copy.200
  22.7 0.5 fusion.25
  23.3 1.5 select_select_fusion
  24.8 2.9 %pad_slice_fusion.3 = (f32[2,3,512,128]{3,2,1,0:T(8,128)}, f32[2,3,512,128]{3,2,1,0:T(8,128)}, f32[2,3,512,128]{3,2,1,0:T(8,128)}, f32[2,3,512,128]{3,2,1,0:T(8,128)}) fusion(f32[2,3,384,128]{3,2,1,0:T(8,128)S(1)} %select_select_fusion), kind=kLoop, calls=%fused_computation.18 | loop fusion | bytes 7471104 | tf_op jit(solution)/shard_map/slice | solution.py:92
  27.8 0.4 select_select_fusion.3
  28.2 0.2 select_select_fusion.4
  28.3 0.2 broadcast_multiply_fusion.1
  28.5 0.6 fusion.91
  29.2 1.0 constant_dynamic-update-slice_fusion.1
  30.1 1.0 constant_dynamic-update-slice_fusion
  36.1 1.1 copy.196
  37.2 0.6 gather_fusion
  40.3 1.1 pad_maximum_fusion.14
  41.4 0.1 fusion.10
  41.5 1.7 collective-permute-start.3
  43.3 0.7 subtract_compare_fusion.14
  44.0 20.4 %collective-permute-done.3 = f32[2,14,16,512]{3,2,1,0:T(8,128)S(1)} collective-permute-done((f32[2,14,16,512]{3,2,1,0:T(8,128)S(1)}, f32[2,14,16,512]{3,2,1,0:T(8,128)S(1)}, u32[]{:S(2)}, u32[]{:S(2)}) %collective-permute-start.3) | collective-permute-done | bytes 917536 | tf_op jit(solution)/shard_map/ppermute | solution.py:21
  64.4 0.2 pad_maximum_fusion.5
  64.6 0.2 reverse_select_fusion.1
  64.8 2.6 %collective-permute-start.4 = (f32[4,14,16,512]{3,2,1,0:T(8,128)S(1)}, f32[4,14,16,512]{3,2,1,0:T(8,128)S(1)}, u32[]{:S(2)}, u32[]{:S(2)}) collective-permute-start(f32[4,14,16,512]{3,2,1,0:T(8,128)S(1)} %bitcast.119), channel_id=1, source_target_pairs={{0,4},{1,5},{2,6},{3,7},{4,0},{5,1},{6,2},{7,3},{8,12},{9,13},{10,... | collective-permute-start | bytes 5505032 | tf_op jit(solution)/shard_map/ppermute | solution.py:21
  67.4 0.4 select_select_fusion.2
  67.8 1.4 select_select_fusion.1
  69.2 3.7 %broadcast_multiply_fusion = f32[2,3,8,32,1056]{4,3,2,1,0:T(8,128)} fusion(f32[2,3,32,1056]{3,2,1,0:T(8,128)S(1)} %select_select_fusion.1, f32[2,3,8,1056]{3,2,1,0:T(8,128)S(1)} %select_select_fusion.2), kind=kLoop, calls=%fused_computation.13 | loop fusion | flops 1622016 | bytes 7501824 | tf_op jit(solution)/shard_map/mul | solution.py:75
  72.9 73.7 %collective-permute-done.4 = f32[4,14,16,512]{3,2,1,0:T(8,128)S(1)} collective-permute-done((f32[4,14,16,512]{3,2,1,0:T(8,128)S(1)}, f32[4,14,16,512]{3,2,1,0:T(8,128)S(1)}, u32[]{:S(2)}, u32[]{:S(2)}) %collective-permute-start.4) | collective-permute-done | bytes 1835040 | tf_op jit(solution)/shard_map/ppermute | solution.py:21
  146.7 0.7 pad_maximum_fusion.4
  147.4 0.8 reverse_select_fusion
  148.2 0.2 copy_bitcast_fusion
  148.4 1.6 fusion.82
  150.1 3.0 %pad_maximum_fusion.1 = f32[22,128,512]{2,1,0:T(8,128)S(1)} fusion(f32[7,128,512]{2,1,0:T(8,128)} %bitcast.122, f32[8,128,512]{2,1,0:T(8,128)} %all-gather.3.cloned.1.call-done, f32[7,128,512]{2,1,0:T(8,128)S(1)} %bitcast.121), kind=kLoop, calls=%fused_computation.3 | loop fusion | flops 2883584 | bytes 11534336 | tf_op jit(solution)/shard_map/concatenate | solution.py:118
  153.1 0.8 constant_dynamic-slice_fusion.1
  153.9 0.5 slice-done.1
  154.4 6.6 %fusion = f32[2,768,512]{2,1,0:T(8,128)S(1)} fusion(f32[2,768,1056]{2,1,0:T(8,128)S(1)} %bitcast.115, f32[1,1056,512]{2,1,0:T(8,128)S(1)} %bitcast.118, f32[1,1056,512]{2,1,0:T(8,128)S(1)} %bitcast.117), kind=kOutput, calls=%fused_computation.5 | convolution fusion | flops 4983914496 | bytes 13959168 | tf_op jit(solution)/shard_map/tmk,tkz->tmz/dot_general | solution.py:134
  161.1 3.3 %bitcast_divide_fusion = f32[2,256,512]{2,1,0:T(8,128)S(1)} fusion(f32[8,2,32,512]{3,2,0,1:T(8,128)S(1)} %copy-done.10, f32[2,3,256,512]{3,2,1,0:T(8,128)S(1)} %bitcast.124, f32[2,3,512,128]{3,2,1,0:T(8,128)S(1)} %copy-done.5, f32[2,3,512,128]{3,2,1,0:T(8,128)S(1)} %copy-done.6, f32[2,3,512,128]{3,2,1,0:T(8,128)S(1)} %copy-done.7, ...), kind=kOutput, calls=%fused_computation.40 | convolution fusion | flops 2420899840 | bytes 11534336 | tf_op jit(solution)/shard_map/tqmz,tqzn->tmn/dot_general | solution.py:136
  164.4 1.5 fusion.92
  165.9 3.0 %fusion.8 = f32[2,256,512]{2,1,0:T(8,128)S(1)} fusion(f32[2,3,256,512]{3,2,1,0:T(8,128)S(1)} %bitcast.116, f32[2,3,512,128]{3,2,1,0:T(8,128)S(1)} %copy-done.5, f32[2,3,512,128]{3,2,1,0:T(8,128)S(1)} %copy-done.6, f32[2,3,512,128]{3,2,1,0:T(8,128)S(1)} %copy-done.7, f32[2,3,512,128]{3,2,1,0:T(8,128)S(1)} %copy-done.4, f32[2]{0:T(128)S(1)} %gather_fusion), kind=kOutput, calls=%fused_computation.38 | convolution fusion | flops 2420899840 | bytes 10485768 | tf_op jit(solution)/shard_map/tqmz,tqnz->tmn/dot_general | solution.py:143
  169.0 0.2 broadcast_in_dim.793
  169.3 0.7 dynamic_update_slice.6
  170.0 0.1 dynamic-slice_add_fusion
  170.2 0.7 dynamic_update_slice.7
  170.9 1.3 copy-done.3
  172.4 11.9 %all-gather = f32[8,2,2]{2,1,0:T(2,128)S(1)} all-gather(f32[1,2,2]{2,1,0:T(2,128)S(1)} %bitcast.211), channel_id=1, replica_groups=mesh['region'=4,'tile'=8] {'tile'}, dimensions={0}, use_global_device_ids=true | all-gather | bytes 144 | tf_op jit(solution)/shard_map/all_gather | solution.py:108
  184.6 25.9 %reduce-scatter.2.cloned.1.call-done = f32[8,16,512]{2,1,0:T(8,128)} async-done(((f32[8,128,512]{2,1,0:T(8,128)}), f32[8,16,512]{2,1,0:T(8,128)}) %reduce-scatter.2.cloned.1.call-update) | async-done | bytes 262160 | tf_op jit(solution)/shard_map/reduce_scatter | solution.py:151
  210.5 1.8 multiply_divide_fusion
  (94 shorter events, 4.2 us)
Async XLA Ops:
  6.5 10.8 %copy-start = (f32[6,3,3,15]{3,2,1,0:T(4,128)S(1)}, f32[6,3,3,15]{3,2,1,0:T(4,128)}, u32[]{:S(2)}) copy-start(f32[6,3,3,15]{3,2,1,0:T(4,128)} %param.10) | copy-start | bytes 9724
  6.5 143.6 %all-gather.3.cloned.1.call-start = ((), (), s32[]{:S(2)}) async-start(), calls=%async_computation.1 | async-start | bytes 2359296 | tf_op jit(solution)/shard_map/all_gather | solution.py:111
  7.3 203.3 %reduce-scatter.2.cloned.1.call-start = ((), (), s32[]{:S(2)}) async-start(), calls=%async_computation.2 | async-start | bytes 2359296 | tf_op jit(solution)/shard_map/reduce_scatter | solution.py:151
  8.4 20.8 %collective-permute-start = (f32[7,16,512]{2,1,0:T(8,128)S(1)}, f32[7,16,512]{2,1,0:T(8,128)}, u32[]{:S(2)}, u32[]{:S(2)}) collective-permute-start(f32[7,16,512]{2,1,0:T(8,128)S(1)} %get-tuple-element.18), channel_id=1, source_target_pairs={{0,8},{8,16},{16,24},{1,9},{9,17},{17,25},{2,10},{10,18},{18,26},{... | collective-permute-start | bytes 688136 | tf_op jit(solution)/shard_map/ppermute | solution.py:113
  13.9 16.2 %collective-permute-start.1 = (f32[7,16,512]{2,1,0:T(8,128)S(1)}, f32[7,16,512]{2,1,0:T(8,128)}, u32[]{:S(2)}, u32[]{:S(2)}) collective-permute-start(f32[7,16,512]{2,1,0:T(8,128)S(1)} %get-tuple-element.17), channel_id=1, source_target_pairs={{8,0},{16,8},{24,16},{9,1},{17,9},{25,17},{10,2},{18,10},{26,18},{... | collective-permute-start | bytes 688136 | tf_op jit(solution)/shard_map/ppermute | solution.py:116
  27.7 8.4 %copy-start.9 = (f32[8,2,32,512]{3,2,1,0:T(8,128)S(1)}, f32[8,2,32,512]{3,2,1,0:T(8,128)}, u32[]{:S(2)}) copy-start(f32[8,2,32,512]{3,2,1,0:T(8,128)} %param.7) | copy-start | bytes 3145732
  28.5 8.6 %copy-start.2 = (f32[6]{0:T(128)S(1)}, f32[6]{0:T(128)}, u32[]{:S(2)}) copy-start(f32[6]{0:T(128)} %param.11) | copy-start | bytes 76
  31.1 9.1 %collective-permute-start.2 = (f32[1,14,16,512]{3,2,1,0:T(8,128)S(1)}, f32[1,14,16,512]{3,2,1,0:T(8,128)}, u32[]{:S(2)}, u32[]{:S(2)}) collective-permute-start(f32[1,14,16,512]{3,2,1,0:T(8,128)S(1)} %bitcast.128), channel_id=1, source_target_pairs={{0,1},{1,0},{2,3},{3,2},{4,5},{5,4},{6,7},{7,6},{8,9},{9,8},{10,11... | collective-permute-start | bytes 1376264 | tf_op jit(solution)/shard_map/ppermute | solution.py:21
  41.5 22.8 %collective-permute-start.3 = (f32[2,14,16,512]{3,2,1,0:T(8,128)S(1)}, f32[2,14,16,512]{3,2,1,0:T(8,128)S(1)}, u32[]{:S(2)}, u32[]{:S(2)}) collective-permute-start(f32[2,14,16,512]{3,2,1,0:T(8,128)S(1)} %get-tuple-element.16), channel_id=1, source_target_pairs={{0,2},{1,3},{2,0},{3,1},{4,6},{5,7},{6,4},{7,5},{8,10},{9,11},{10,... | collective-permute-start | bytes 2752520 | tf_op jit(solution)/shard_map/ppermute | solution.py:21
  64.8 81.9 %collective-permute-start.4 = (f32[4,14,16,512]{3,2,1,0:T(8,128)S(1)}, f32[4,14,16,512]{3,2,1,0:T(8,128)S(1)}, u32[]{:S(2)}, u32[]{:S(2)}) collective-permute-start(f32[4,14,16,512]{3,2,1,0:T(8,128)S(1)} %bitcast.119), channel_id=1, source_target_pairs={{0,4},{1,5},{2,6},{3,7},{4,0},{5,1},{6,2},{7,3},{8,12},{9,13},{10,... | collective-permute-start | bytes 5505032 | tf_op jit(solution)/shard_map/ppermute | solution.py:21
  150.1 3.8 %slice-start = ((s8[7077888]{0:T(1024)(128)(4,1)}), s8[4194304]{0:T(1024)(128)(4,1)S(1)}, s32[]{:S(2)}) async-start(s8[7077888]{0:T(1024)(128)(4,1)} %bitcast.113), calls=%async_computation.3 | async-start | bytes 8388608
  150.1 4.3 %slice-start.1 = ((s8[7077888]{0:T(1024)(128)(4,1)}), s8[2883584]{0:T(1024)(128)(4,1)S(1)}, s32[]{:S(2)}) async-start(s8[7077888]{0:T(1024)(128)(4,1)} %bitcast.113), calls=%async_computation.4 | async-start | bytes 5767168
  154.4 6.7 %copy-start.4 = (f32[2,3,512,128]{3,2,1,0:T(8,128)S(1)}, f32[2,3,512,128]{3,2,1,0:T(8,128)}, u32[]{:S(2)}) copy-start(f32[2,3,512,128]{3,2,1,0:T(8,128)} %get-tuple-element.9) | copy-start | bytes 4718596
  154.4 6.7 %copy-start.5 = (f32[2,3,512,128]{3,2,1,0:T(8,128)S(1)}, f32[2,3,512,128]{3,2,1,0:T(8,128)}, u32[]{:S(2)}) copy-start(f32[2,3,512,128]{3,2,1,0:T(8,128)} %get-tuple-element.10) | copy-start | bytes 4718596
  154.4 6.7 %copy-start.6 = (f32[2,3,512,128]{3,2,1,0:T(8,128)S(1)}, f32[2,3,512,128]{3,2,1,0:T(8,128)}, u32[]{:S(2)}) copy-start(f32[2,3,512,128]{3,2,1,0:T(8,128)} %get-tuple-element.11) | copy-start | bytes 4718596
  154.4 6.7 %copy-start.7 = (f32[2,3,512,128]{3,2,1,0:T(8,128)S(1)}, f32[2,3,512,128]{3,2,1,0:T(8,128)}, u32[]{:S(2)}) copy-start(f32[2,3,512,128]{3,2,1,0:T(8,128)} %get-tuple-element.12) | copy-start | bytes 4718596
  154.4 6.7 %copy-start.10 = (f32[8,2,32,512]{3,2,0,1:T(8,128)S(1)}, f32[8,2,32,512]{3,2,0,1:T(8,128)}, u32[]{:S(2)}) copy-start(f32[8,2,32,512]{3,2,0,1:T(8,128)} %copy.196) | copy-start | bytes 3145732
  170.0 42.3 %copy-start.1 = (f32[6,3,3,15]{3,2,1,0:T(4,128)S(1)}, f32[6,3,3,15]{3,2,1,0:T(4,128)}, u32[]{:S(2)}) copy-start(f32[6,3,3,15]{3,2,1,0:T(4,128)} %param.10) | copy-start | bytes 9724
  170.1 40.4 %copy-start.8 = (f32[8,16,512]{2,1,0:T(8,128)S(1)}, f32[8,16,512]{2,1,0:T(8,128)}, u32[]{:S(2)}) copy-start(f32[8,16,512]{2,1,0:T(8,128)} %param.6) | copy-start | bytes 786436
  170.9 1.4 copy-start.3
Sparse Core Ops, SparseCore 0:
  9.0 31.9 all-gather.2
  172.4 38.0 reduce-scatter.1
